TPU v7x, 512 devices: a whole 4x8x8 slice. The times are simulated.
512 devices in a mesh: ctx: 32 (over z, x), tp: 16 (over y, core).
Axes of the slice: x: 4, y: 8, z: 8, core: 2. Of those that a mesh axis runs over, the one named last changes fastest.
Arguments:
- hidden: bfloat16 [8192, 2048], P(('ctx', 'tp')), may hold values from -14 to 14
- in_weight: bfloat16 [2048, 2, 4096], P(None, None, 'tp'), may hold values from -0.125 to 0.125
- step_weight: bfloat16 [2048, 64], P(None, 'tp'), may hold values from -0.125 to 0.125
- group_weight: bfloat16 [256, 4, 2048], P('tp'), may hold values from -0.125 to 0.125
- conv_inner: float32 [4, 4096], P(None, 'tp'), may hold values from -3 to 3
- inner_bias: float32 [4096], P('tp'), may hold values from -2.5 to 2.5
- conv_group: float32 [4, 1024], replicated, may hold values from -3 to 3
- group_bias: float32 [1024], replicated, may hold values from -2.5 to 2.5
- step_bias: float32 [64], P('tp'), may hold values from -9.5 to 0
- log_rate: float32 [64], P('tp'), may hold values from -2.5 to -0.5
- skip_weight: float32 [64], P('tp'), may hold values from 0.25 to 1
- norm_gain: float32 [4096], P('tp'), may hold values from 0.1 to 1.9
- out_weight: bfloat16 [4096, 2048], P('tp'), may hold values from -0.09375 to 0.09375
Outputs:
- mixed: bfloat16 [8192, 2048], P(('ctx', 'tp'))
All inputs are finite; a program needn't handle non-finite values.
Results may differ from a plain program's by a relative error of at most 0.024.
Values may be sent and summed in bfloat16 or wider, within the bound.
No kernel may reach another device: no remote copies, remote signals or barrier semaphores. Data moves between devices by JAX's collectives and lax.ppermute only.
A program may use at most 64 MiB of HBM per device.

v0:
```python
import jax
import jax.numpy as jnp
from jax import lax
from jax.sharding import PartitionSpec as P

HEADS = 64
HEAD_DIM = 64
STATE = 128
GROUPS = 4
BLOCK = 256
KERNEL = 4


def shifted(x, axis, by):
    peers = lax.axis_size(axis)
    pairs = [(i, i + by) for i in range(peers) if 0 <= i + by < peers]
    return lax.ppermute(x, axis, pairs)


def entering(x, axis, combine, identity):
    peers, place = (lax.axis_size(axis), lax.axis_index(axis))
    everything = jax.tree.map(lambda part: lax.all_gather(part, axis), x)
    start = jax.tree.map(
        lambda part, zero: jnp.broadcast_to(jnp.asarray(zero, part.dtype), part.shape), x, identity
    )

    def turn(k, before):
        reached = k < place
        new = combine(before, jax.tree.map(lambda part: part[k], everything))
        return jax.tree.map(lambda a, b: jnp.where(reached, a, b), new, before)

    return lax.fori_loop(0, peers, turn, start)


def causal_conv(prior_rows, raw_rows, conv_weight, conv_bias):
    joined = jnp.concatenate([prior_rows, raw_rows], axis=0).astype(jnp.float32)
    length = raw_rows.shape[0]
    running = jnp.broadcast_to(conv_bias[None, :], raw_rows.shape)
    for offset in range(conv_weight.shape[0]):
        running = running + conv_weight[offset][None, :] * joined[offset : offset + length]
    return jax.nn.silu(running).astype(jnp.bfloat16)


def combine_states(earlier, latter):
    return (earlier[0] * latter[0], latter[0][:, None, None] * earlier[1] + latter[1])


def body(
    hidden,
    in_weight,
    step_weight,
    group_weight,
    conv_inner,
    inner_bias,
    conv_group,
    group_bias,
    step_bias,
    log_rate,
    skip_weight,
    norm_gain,
    out_weight,
):
    heads_dev = log_rate.shape[0]
    inner_dev = in_weight.shape[2]
    group_cols = 2 * STATE
    group_index = lax.axis_index("tp") * heads_dev // (HEADS // GROUPS)
    zx_weight = in_weight.reshape(in_weight.shape[0], 2 * inner_dev)
    full_weight = lax.all_gather(group_weight, "tp", axis=0, tiled=True)
    map_weight = lax.dynamic_slice_in_dim(full_weight, group_index, 1, 1)[:, 0, :]
    shard_rows = lax.all_gather(hidden, "tp", axis=0, tiled=True)
    projected = jnp.concatenate(
        [
            jnp.dot(shard_rows, zx_weight, preferred_element_type=jnp.float32),
            lax.dot_general(
                shard_rows, map_weight, (((1,), (1,)), ((), ())), preferred_element_type=jnp.float32
            ),
            jnp.dot(shard_rows, step_weight, preferred_element_type=jnp.float32),
        ],
        axis=1,
    ).astype(jnp.bfloat16)
    gate_raw = projected[:, :inner_dev]
    inner_raw = projected[:, inner_dev : 2 * inner_dev]
    map_part = projected[:, 2 * inner_dev : projected.shape[1] - heads_dev]
    step_raw = projected[:, projected.shape[1] - heads_dev :]
    border_rows = KERNEL - 1
    length = inner_raw.shape[0]
    inner_prior, map_prior = shifted(
        (inner_raw[length - border_rows :], map_part[length - border_rows :]), "ctx", 1
    )
    x_conv = causal_conv(inner_prior, inner_raw, conv_inner, inner_bias)
    own_taps = lax.dynamic_slice_in_dim(conv_group, group_index * group_cols, group_cols, 1)
    own_bias = lax.dynamic_slice_in_dim(group_bias, group_index * group_cols, group_cols, 0)
    maps = causal_conv(map_prior, map_part, own_taps, own_bias)
    step_size = jax.nn.softplus(step_raw.astype(jnp.float32) + step_bias[None, :])
    decay_rate = -jnp.exp(log_rate)
    blocks = length // BLOCK
    x_blocks = x_conv.reshape(blocks, BLOCK, heads_dev, HEAD_DIM)
    input_map = maps[:, :STATE].reshape(blocks, BLOCK, STATE)
    output_map = maps[:, STATE:].reshape(blocks, BLOCK, STATE)
    step_blocks = jnp.swapaxes(step_size.reshape(blocks, BLOCK, heads_dev), 1, 2)
    cumulative = jnp.cumsum(step_blocks * decay_rate[None, :, None], axis=2)
    scores = jnp.einsum("kin,kjn->kij", output_map, input_map, preferred_element_type=jnp.float32)
    causal = jnp.arange(BLOCK)[:, None] >= jnp.arange(BLOCK)[None, :]
    exponent = jnp.where(causal, cumulative[..., :, None] - cumulative[..., None, :], -jnp.inf)
    mixing = (scores[:, None] * jnp.exp(exponent) * step_blocks[..., None, :]).astype(jnp.bfloat16)
    within = jnp.einsum("khij,kjhp->kihp", mixing, x_blocks, preferred_element_type=jnp.float32)
    weight = jnp.exp(cumulative[..., BLOCK - 1 :] - cumulative) * step_blocks
    x_float = x_blocks.astype(jnp.float32)
    weighted = (x_float * jnp.swapaxes(weight, 1, 2)[..., None]).astype(jnp.bfloat16)
    block_state = jnp.einsum(
        "kjhp,kjn->khpn", weighted, input_map, preferred_element_type=jnp.float32
    )
    block_decay = jnp.exp(cumulative[..., BLOCK - 1])

    def advance(carry, item):
        running, product = carry
        block_stop_index, state_here = item
        return (
            (block_stop_index[:, None, None] * running + state_here, product * block_stop_index),
            (running, product),
        )

    empty_state = jnp.zeros((heads_dev, HEAD_DIM, STATE), jnp.float32)
    (dev_state, dev_decay), (local_starts, prefixes) = lax.scan(
        advance, (empty_state, jnp.ones((heads_dev,), jnp.float32)), (block_decay, block_state)
    )
    decay_in, incoming = entering(
        (dev_decay, dev_state),
        "ctx",
        combine_states,
        (jnp.ones_like(dev_decay), jnp.zeros_like(dev_state)),
    )
    starting = local_starts + prefixes[:, :, None, None] * incoming[None]
    carried = jnp.einsum(
        "kin,khpn->kihp",
        output_map,
        starting.astype(jnp.bfloat16),
        preferred_element_type=jnp.float32,
    )
    carried = carried * jnp.swapaxes(jnp.exp(cumulative), 1, 2)[..., None]
    result_heads = within + carried + skip_weight[None, None, :, None] * x_float
    result_heads = result_heads.reshape(length, inner_dev)
    gated = result_heads * jax.nn.silu(gate_raw.astype(jnp.float32))
    squares = jnp.sum(gated * gated, axis=1)
    own_slot = (jnp.arange(GROUPS) == group_index)[:, None]
    group_sums = lax.psum(jnp.where(own_slot, squares[None, :], 0.0), "tp")
    own_total = jnp.sum(jnp.where(own_slot, group_sums, 0.0), axis=0)
    inverse = lax.rsqrt(own_total / (HEADS * HEAD_DIM // GROUPS) + 1e-05)
    normed = (gated * inverse[:, None] * norm_gain[None, :]).astype(jnp.bfloat16)
    mixed = lax.psum_scatter(
        jnp.dot(normed, out_weight, preferred_element_type=jnp.float32),
        "tp",
        scatter_dimension=0,
        tiled=True,
    )
    return mixed.astype(jnp.bfloat16)


def solution(mesh):
    placed = (
        P(("ctx", "tp"), None),
        P(None, None, "tp"),
        P(None, "tp"),
        P("tp", None, None),
        P(None, "tp"),
        P("tp"),
        P(),
        P(),
        P("tp"),
        P("tp"),
        P("tp"),
        P("tp"),
        P("tp", None),
    )
    return jax.shard_map(
        body, mesh=mesh, in_specs=placed, out_specs=P(("ctx", "tp"), None), check_vma=False
    )
```

profile of v0, /device:TPU:27, one launch (start us, length us, event | category | flops | bytes accessed | tf_op | source)
XLA Modules:
  0.0 323.9 jit_solution(4867282855328708421)
XLA Ops:
  7.3 1.8 copy.45
  9.3 2.1 copy.56
  13.1 41.7 %all-gather.6.cloned.1.call-done = bf16[256,2048]{1,0:T(8,128)(2,1)} async-done(((bf16[16,2048]{1,0:T(8,128)(2,1)}), bf16[256,2048]{1,0:T(8,128)(2,1)}) %all-gather.6.cloned.1.call-update) | async-done | bytes 1048592 | tf_op jit(solution)/shard_map/all_gather | solution.py:70
  54.8 1.6 bitcast_multiply_fusion.1
  56.4 1.2 reduce-window.6
  58.1 1.9 convolution_convert_fusion
  60.1 3.1 collective-permute-start
  64.4 35.8 %all-gather.8.cloned.1.call-done = bf16[256,4,2048]{2,0,1:T(8,128)(2,1)} async-done(((bf16[16,4,2048]{2,0,1:T(8,128)(2,1)}), bf16[256,4,2048]{2,0,1:T(8,128)(2,1)}) %all-gather.8.cloned.1.call-update) | async-done | bytes 4194320 | tf_op jit(solution)/shard_map/all_gather | solution.py:68
  100.3 2.0 fusion.4
  102.3 3.1 collective-permute-start.1
  107.9 34.2 %all-gather = f32[32,4,1]{1,2,0:T(1,128)S(1)} all-gather(f32[1,4,1]{1,2,0:T(1,128)S(1)} %copy.48), channel_id=2, replica_groups=mesh['ctx'=32,'tp'=16] {'ctx'}, dimensions={0}, use_global_device_ids=true | all-gather | bytes 528 | tf_op jit(solution)/shard_map/all_gather | solution.py:22
  142.6 49.1 %all-gather.10.cloned.1.call-done = f32[128,64,128]{2,1,0:T(8,128)} async-done(((f32[4,64,128]{2,1,0:T(8,128)}), f32[128,64,128]{2,1,0:T(8,128)}) %all-gather.10.cloned.1.call-update) | async-done | bytes 4194320 | tf_op jit(solution)/shard_map/all_gather | solution.py:22
  191.7 33.1 %while.9 = (s32[]{:T(128)}, f32[4,64,128]{2,1,0:T(8,128)S(1)}, s32[]{:T(128)}, f32[32,4]{1,0:T(8,128)S(1)}, f32[32,4,64,128]{3,2,1,0:T(8,128)}, /*index=5*/s32[]{:T(128)}, s32[]{:T(128)}) while((s32[]{:T(128)}, f32[4,64,128]{2,1,0:T(8,128)S(1)}, s32[]{:T(128)}, f32[32,4]{1,0:T(8,128)S(1)}, f32[32,4,64,128]{3,2,1,0:T(8,128)}, ...), condition=%wide.region_3.4_spmd.clone, body=%wide.region_2.3_spmd.clone.sunk | while | flops 131076 | bytes 393369 | solution.py:32
  192.7 1.0 fusion.52
  193.8 1.0 fusion.52
  194.8 1.0 fusion.52
  195.8 1.0 fusion.52
  196.9 1.0 fusion.52
  197.9 1.0 fusion.52
  198.9 1.0 fusion.52
  200.0 1.0 fusion.52
  201.0 1.0 fusion.52
  202.0 1.0 fusion.52
  203.1 1.0 fusion.52
  204.1 1.0 fusion.52
  205.1 1.0 fusion.52
  206.2 1.0 fusion.52
  207.2 1.0 fusion.52
  225.8 26.8 %psum.7 = f32[4,256]{1,0:T(4,128)S(1)} all-reduce(f32[4,256]{1,0:T(4,128)S(1)} %broadcast_select_fusion), channel_id=1, replica_groups=mesh['ctx'=32,'tp'=16] {'tp'}, use_global_device_ids=true, to_apply=%region_5.6 | all-reduce | flops 1024 | bytes 8192 | tf_op jit(solution)/shard_map/psum | solution.py:146
  252.8 1.8 fusion.27
  254.7 61.1 %reduce-scatter.2.cloned.1.call-done = f32[16,2048]{1,0:T(8,128)} async-done(((f32[256,2048]{1,0:T(8,128)}), f32[16,2048]{1,0:T(8,128)}) %reduce-scatter.2.cloned.1.call-update) | async-done | bytes 131088 | tf_op jit(solution)/shard_map/reduce_scatter | solution.py:150
  315.8 1.5 convert_element_type.77
  (119 shorter events, 25.4 us)
Async XLA Ops:
  6.5 246.2 %copy-start = (bf16[256,2048]{1,0:T(8,128)(2,1)S(1)}, bf16[256,2048]{1,0:T(8,128)(2,1)}, u32[]{:S(2)}) copy-start(bf16[256,2048]{1,0:T(8,128)(2,1)} %param.27) | copy-start | bytes 3145732
  6.5 48.3 %all-gather.6.cloned.1.call-start = ((), (), s32[]{:S(2)}) async-start(), calls=%async_computation.1 | async-start | bytes 1114112 | tf_op jit(solution)/shard_map/all_gather | solution.py:70
  7.3 93.0 %all-gather.8.cloned.1.call-start = ((), (), s32[]{:S(2)}) async-start(), calls=%async_computation.2 | async-start | bytes 4456448 | tf_op jit(solution)/shard_map/all_gather | solution.py:68
  9.2 182.5 %all-gather.10.cloned.1.call-start = ((), (), s32[]{:S(2)}) async-start(), calls=%async_computation.4 | async-start | bytes 4325376 | tf_op jit(solution)/shard_map/all_gather | solution.py:22
  9.2 3.8 %copy-start.5 = (f32[4]{0:T(128)S(1)}, f32[4]{0:T(128)}, u32[]{:S(2)}) copy-start(f32[4]{0:T(128)} %param.24) | copy-start | bytes 52
  9.2 3.8 %copy-start.1 = (f32[4,256]{1,0:T(4,128)S(1)}, f32[4,256]{1,0:T(4,128)}, u32[]{:S(2)}) copy-start(f32[4,256]{1,0:T(4,128)} %param.19) | copy-start | bytes 12292
  9.3 45.5 %copy-start.4 = (bf16[2048,4]{0,1:T(4,128)(2,1)S(1)}, bf16[2048,4]{0,1:T(4,128)(2,1)}, u32[]{:S(2)}) copy-start(bf16[2048,4]{0,1:T(4,128)(2,1)} %param.17) | copy-start | bytes 49156
  9.3 45.5 %copy-start.6 = (f32[4]{0:T(128)S(1)}, f32[4]{0:T(128)}, u32[]{:S(2)}) copy-start(f32[4]{0:T(128)} %param.23) | copy-start | bytes 52
  60.0 45.4 %copy-start.3 = (f32[256]{0:T(256)S(1)}, f32[256]{0:T(256)}, u32[]{:S(2)}) copy-start(f32[256]{0:T(256)} %param.20) | copy-start | bytes 3076
  60.1 4.3 %collective-permute-start = (bf16[3,256]{1,0:T(4,128)(2,1)S(1)}, bf16[3,256]{1,0:T(4,128)(2,1)S(1)}, u32[]{:S(2)}, u32[]{:S(2)}) collective-permute-start(bf16[3,256]{1,0:T(4,128)(2,1)S(1)} %slice.112), channel_id=1, source_target_pairs={{0,16},{16,32},{32,48},{48,64},{64,80},{80,96},{96,112},{112,128},... | collective-permute-start | bytes 4616 | tf_op jit(solution)/shard_map/ppermute | solution.py:17
  102.3 4.3 %collective-permute-start.1 = (bf16[3,256]{1,0:T(4,128)(2,1)S(1)}, bf16[3,256]{1,0:T(4,128)(2,1)S(1)}, u32[]{:S(2)}, u32[]{:S(2)}) collective-permute-start(bf16[3,256]{1,0:T(4,128)(2,1)S(1)} %slice.118), channel_id=1, source_target_pairs={{0,16},{16,32},{32,48},{48,64},{64,80},{80,96},{96,112},{112,128},... | collective-permute-start | bytes 4616 | tf_op jit(solution)/shard_map/ppermute | solution.py:17
  106.8 118.1 %copy-start.7 = (f32[4]{0:T(128)S(1)}, f32[4]{0:T(128)}, u32[]{:S(2)}) copy-start(f32[4]{0:T(128)} %param.25) | copy-start | bytes 52
  107.7 208.1 %reduce-scatter.2.cloned.1.call-start = ((), (), s32[]{:S(2)}) async-start(), calls=%async_computation.3 | async-start | bytes 2228224 | tf_op jit(solution)/shard_map/reduce_scatter | solution.py:150
  224.8 28.0 %copy-start.2 = (f32[256]{0:T(256)S(1)}, f32[256]{0:T(256)}, u32[]{:S(2)}) copy-start(f32[256]{0:T(256)} %param.26) | copy-start | bytes 3076
Sparse Core Ops, SparseCore 0:
  9.5 45.2 all-gather.5
  56.9 43.2 all-gather.7
  107.8 83.8 all-gather.9
  254.8 60.9 reduce-scatter.1
where the time goes:
time: 325 us; the launch traced here: 324 us
  waiting for transfers between devices  190 us (58%)
  blocking collectives  61.1 us (19%)
  other arithmetic  35.5 us (11%)
  between operations  13.5 us (4%)
  matrix products  9.08 us (3%)
  local copies, waits for them, and re-layouts  7.25 us (2%)
  starting transfers between devices  6.32 us (2%)
    reduce_scatter x1, waiting for transfers between devices, body(): lax.psum_scatter(jnp.dot(normed, out_weight, preferred_element_type=jnp.f...  61.1 us
    all_gather x1, waiting for transfers between devices, entering(): everything = jax.tree.map(lambda part: lax.all_gather(part, axis), x)  49.1 us
    all_gather x1, waiting for transfers between devices, body(): shard_rows = lax.all_gather(hidden, 'tp', axis=0, tiled=True)  41.7 us
    all_gather x1, waiting for transfers between devices, body(): full_weight = lax.all_gather(group_weight, 'tp', axis=0, tiled=True)  35.8 us
    all_gather x1, blocking collectives, entering(): everything = jax.tree.map(lambda part: lax.all_gather(part, axis), x)  34.2 us
    select_n x32, other arithmetic, turn(): return jax.tree.map(lambda a, b: jnp.where(reached, a, b), new, before)  31.8 us
    psum x1, blocking collectives, body(): group_sums = lax.psum(jnp.where(own_slot, squares[None, :], 0.0), 'tp')  26.8 us
  transfers between devices with their start and end apart: 6, of which 6 were waited for; matrix products, arithmetic and copies ran while one was open for 4% of the time, Pallas kernels for 0%

commit v1 on v0

--- a/solution.py
+++ b/solution.py
@@ -67,7 +67,28 @@
     zx_weight = in_weight.reshape(in_weight.shape[0], 2 * inner_dev)
     full_weight = lax.all_gather(group_weight, "tp", axis=0, tiled=True)
     map_weight = lax.dynamic_slice_in_dim(full_weight, group_index, 1, 1)[:, 0, :]
-    shard_rows = lax.all_gather(hidden, "tp", axis=0, tiled=True)
+    parts_out = lax.axis_size("tp")
+    base_arr, d_next, row_out = (parts_out, lax.axis_index("tp"), hidden.shape[0])
+    pool = []
+    for w in [*range(base_arr)]:
+        pool.append((w, (w + 1) % base_arr))
+    gallery = []
+    for w in [*range(base_arr)]:
+        gallery.append((w, (w - 1) % base_arr))
+    shard_rows = jnp.zeros((*hidden.shape[:0], base_arr * row_out, *hidden.shape[1:]), hidden.dtype)
+    shard_rows = lax.dynamic_update_slice_in_dim(shard_rows, hidden, d_next * row_out, axis=0)
+    state_next = extra = hidden
+    r2 = base_arr // 2
+    for h in [*range(1, r2 + 1)]:
+        state_next = lax.ppermute(state_next, "tp", pool)
+        shard_rows = lax.dynamic_update_slice_in_dim(
+            shard_rows, state_next, (d_next - h) % base_arr * row_out, axis=0
+        )
+        if h < base_arr - r2:
+            extra = lax.ppermute(extra, "tp", gallery)
+            shard_rows = lax.dynamic_update_slice_in_dim(
+                shard_rows, extra, (d_next + h) % base_arr * row_out, axis=0
+            )
     projected = jnp.concatenate(
         [
             jnp.dot(shard_rows, zx_weight, preferred_element_type=jnp.float32),

time: 325 us -> 299 us (0.920)
  waiting for transfers between devices: 190 us -> 129 us
  starting transfers between devices: 6.32 us -> 34.2 us
  blocking collectives: 61.1 us -> 67.7 us
    all_gather x1 -> x0, waiting for transfers between devices: 41.7 us -> none  [body(): shard_rows = lax.all_gather(hidden, 'tp', axis=0, tiled=True)]
    all_gather x1, waiting for transfers between devices: 35.8 us -> 0.02 us  [body(): full_weight = lax.all_gather(group_weight, 'tp', axis=0, tiled=True)]
    ppermute x0 -> x15, starting transfers between devices: none -> 27.7 us  [the longest x8 27.7 us: body(): state_next = lax.ppermute(state_next, 'tp', pool)]
    ppermute x0 -> x15, waiting for transfers between devices: none -> 12.9 us  [the longest x7 6.92 us: body(): extra = lax.ppermute(extra, 'tp', gallery)]
    all_gather x1, blocking collectives: 34.2 us -> 40.9 us  [entering(): everything = jax.tree.map(lambda part: lax.all_gather(part, axis), x)]
    all_gather x1, waiting for transfers between devices: 49.1 us -> 53.7 us  [entering(): everything = jax.tree.map(lambda part: lax.all_gather(part, axis), x)]
  transfers between devices with their start and end apart: 6 -> 20, of which waited for: 6 -> 13; matrix products, arithmetic and copies ran while one was open for 4% -> 4% of each run, Pallas kernels for 0% -> 0%
where the time goes in v1:
time: 299 us; the launch traced here: 298 us
  waiting for transfers between devices  129 us (43%)
  blocking collectives  67.7 us (23%)
  other arithmetic  35.5 us (12%)
  starting transfers between devices  34.2 us (11%)
  between operations  13.5 us (5%)
  local copies, waits for them, and re-layouts  9 us (3%)
  matrix products  7.89 us (3%)
    reduce_scatter x1, waiting for transfers between devices, body(): lax.psum_scatter(jnp.dot(normed, out_weight, preferred_element_type=jnp.f...  61.1 us
    all_gather x1, waiting for transfers between devices, entering(): everything = jax.tree.map(lambda part: lax.all_gather(part, axis), x)  53.7 us
    all_gather x1, blocking collectives, entering(): everything = jax.tree.map(lambda part: lax.all_gather(part, axis), x)  40.9 us
    select_n x32, other arithmetic, turn(): return jax.tree.map(lambda a, b: jnp.where(reached, a, b), new, before)  31.8 us
    ppermute x8, starting transfers between devices, body(): state_next = lax.ppermute(state_next, 'tp', pool)  27.7 us
    psum x1, blocking collectives, body(): group_sums = lax.psum(jnp.where(own_slot, squares[None, :], 0.0), 'tp')  26.8 us
    ppermute x7, waiting for transfers between devices, body(): extra = lax.ppermute(extra, 'tp', gallery)  6.92 us
    ppermute x2, starting transfers between devices, shifted(): return lax.ppermute(x, axis, pairs)  6.39 us
  transfers between devices with their start and end apart: 20, of which 13 were waited for; matrix products, arithmetic and copies ran while one was open for 4% of the time, Pallas kernels for 0%

profile of v1, /device:TPU:27, one launch (start us, length us, event | category | flops | bytes accessed | tf_op | source)
XLA Modules:
  0.0 297.9 jit_solution(16449089013121062387)
XLA Ops:
  6.5 1.9 copy.45
  8.5 3.1 %collective-permute-start = (bf16[16,2048]{1,0:T(8,128)(2,1)}, bf16[16,2048]{1,0:T(8,128)(2,1)S(1)}, u32[]{:S(2)}, u32[]{:S(2)}) collective-permute-start(bf16[16,2048]{1,0:T(8,128)(2,1)} %param.15), channel_id=1, source_target_pairs={{0,1},{1,2},{2,3},{3,4},{4,5},{5,6},{6,7},{7,8},{8,9},{9,10},{10,1... | collective-permute-start | bytes 196616 | tf_op jit(solution)/shard_map/ppermute | solution.py:83
  11.6 3.4 %copy.56 = bf16[256,8,2,256]{3,1,2,0:T(8,128)(2,1)} copy(bf16[256,8,2,256]{3,2,1,0:T(2,128)(2,1)} %bitcast.82) | data formatting | bytes 4194304
  16.9 3.0 collective-permute-start.2
  19.9 1.3 collective-permute-done.2
  21.2 3.6 %collective-permute-start.4 = (bf16[16,2048]{1,0:T(8,128)(2,1)S(1)}, bf16[16,2048]{1,0:T(8,128)(2,1)S(1)}, u32[]{:S(2)}, u32[]{:S(2)}) collective-permute-start(bf16[16,2048]{1,0:T(8,128)(2,1)S(1)} %collective-permute-done.2), channel_id=1, source_target_pairs={{0,1},{1,2},{2,3},{3,4},{4,5},{5,6},{6,7},{7,8},{8,9},{9,10},{10,1... | collective-permute-start | bytes 196616 | tf_op jit(solution)/shard_map/ppermute | solution.py:83
  24.8 1.3 collective-permute-done.4
  26.1 3.6 %collective-permute-start.6 = (bf16[16,2048]{1,0:T(8,128)(2,1)S(1)}, bf16[16,2048]{1,0:T(8,128)(2,1)S(1)}, u32[]{:S(2)}, u32[]{:S(2)}) collective-permute-start(bf16[16,2048]{1,0:T(8,128)(2,1)S(1)} %collective-permute-done.4), channel_id=1, source_target_pairs={{0,1},{1,2},{2,3},{3,4},{4,5},{5,6},{6,7},{7,8},{8,9},{9,10},{10,1... | collective-permute-start | bytes 196616 | tf_op jit(solution)/shard_map/ppermute | solution.py:83
  29.7 2.4 collective-permute-done.6
  32.2 3.7 %collective-permute-start.8 = (bf16[16,2048]{1,0:T(8,128)(2,1)S(1)}, bf16[16,2048]{1,0:T(8,128)(2,1)S(1)}, u32[]{:S(2)}, u32[]{:S(2)}) collective-permute-start(bf16[16,2048]{1,0:T(8,128)(2,1)S(1)} %collective-permute-done.6), channel_id=1, source_target_pairs={{0,1},{1,2},{2,3},{3,4},{4,5},{5,6},{6,7},{7,8},{8,9},{9,10},{10,1... | collective-permute-start | bytes 196616 | tf_op jit(solution)/shard_map/ppermute | solution.py:83
  37.2 3.8 %collective-permute-start.10 = (bf16[16,2048]{1,0:T(8,128)(2,1)S(1)}, bf16[16,2048]{1,0:T(8,128)(2,1)S(1)}, u32[]{:S(2)}, u32[]{:S(2)}) collective-permute-start(bf16[16,2048]{1,0:T(8,128)(2,1)S(1)} %collective-permute-done.8), channel_id=1, source_target_pairs={{0,1},{1,2},{2,3},{3,4},{4,5},{5,6},{6,7},{7,8},{8,9},{9,10},{10,1... | collective-permute-start | bytes 196616 | tf_op jit(solution)/shard_map/ppermute | solution.py:83
  41.0 2.0 collective-permute-done.9
  43.1 3.7 %collective-permute-start.12 = (bf16[16,2048]{1,0:T(8,128)(2,1)S(1)}, bf16[16,2048]{1,0:T(8,128)(2,1)S(1)}, u32[]{:S(2)}, u32[]{:S(2)}) collective-permute-start(bf16[16,2048]{1,0:T(8,128)(2,1)S(1)} %collective-permute-done.10), channel_id=1, source_target_pairs={{0,1},{1,2},{2,3},{3,4},{4,5},{5,6},{6,7},{7,8},{8,9},{9,10},{10,1... | collective-permute-start | bytes 196616 | tf_op jit(solution)/shard_map/ppermute | solution.py:83
  46.8 2.3 collective-permute-done.11
  49.2 3.3 %collective-permute-start.14 = (bf16[16,2048]{1,0:T(8,128)(2,1)S(1)}, bf16[16,2048]{1,0:T(8,128)(2,1)S(1)}, u32[]{:S(2)}, u32[]{:S(2)}) collective-permute-start(bf16[16,2048]{1,0:T(8,128)(2,1)S(1)} %collective-permute-done.12), channel_id=1, source_target_pairs={{0,1},{1,2},{2,3},{3,4},{4,5},{5,6},{6,7},{7,8},{8,9},{9,10},{10,1... | collective-permute-start | bytes 196616 | tf_op jit(solution)/shard_map/ppermute | solution.py:83
  52.5 2.1 collective-permute-done.13
  55.2 1.2 reduce-window.6
  56.7 2.3 convolution_convert_fusion
  59.1 3.2 %collective-permute-start.15 = (bf16[3,256]{1,0:T(4,128)(2,1)S(1)}, bf16[3,256]{1,0:T(4,128)(2,1)S(1)}, u32[]{:S(2)}, u32[]{:S(2)}) collective-permute-start(bf16[3,256]{1,0:T(4,128)(2,1)S(1)} %slice.115), channel_id=1, source_target_pairs={{0,16},{16,32},{32,48},{48,64},{64,80},{80,96},{96,112},{112,128},... | collective-permute-start | bytes 4616 | tf_op jit(solution)/shard_map/ppermute | solution.py:17
  63.5 1.7 convolution_convert_fusion.1
  65.2 3.2 %collective-permute-start.16 = (bf16[3,256]{1,0:T(4,128)(2,1)S(1)}, bf16[3,256]{1,0:T(4,128)(2,1)S(1)}, u32[]{:S(2)}, u32[]{:S(2)}) collective-permute-start(bf16[3,256]{1,0:T(4,128)(2,1)S(1)} %slice.121), channel_id=1, source_target_pairs={{0,16},{16,32},{32,48},{48,64},{64,80},{80,96},{96,112},{112,128},... | collective-permute-start | bytes 4616 | tf_op jit(solution)/shard_map/ppermute | solution.py:17
  70.8 40.9 %all-gather = f32[32,4,1]{1,2,0:T(1,128)S(1)} all-gather(f32[1,4,1]{1,2,0:T(1,128)S(1)} %copy.48), channel_id=2, replica_groups=mesh['ctx'=32,'tp'=16] {'ctx'}, dimensions={0}, use_global_device_ids=true | all-gather | bytes 528 | tf_op jit(solution)/shard_map/all_gather | solution.py:22
  112.1 53.7 %all-gather.7.cloned.1.call-done = f32[128,64,128]{2,1,0:T(8,128)} async-done(((f32[4,64,128]{2,1,0:T(8,128)}), f32[128,64,128]{2,1,0:T(8,128)}) %all-gather.7.cloned.1.call-update) | async-done | bytes 4194320 | tf_op jit(solution)/shard_map/all_gather | solution.py:22
  165.8 33.0 %while.9 = (s32[]{:T(128)}, f32[4,64,128]{2,1,0:T(8,128)S(1)}, s32[]{:T(128)}, f32[32,4]{1,0:T(8,128)S(1)}, f32[32,4,64,128]{3,2,1,0:T(8,128)}, /*index=5*/s32[]{:T(128)}, s32[]{:T(128)}) while((s32[]{:T(128)}, f32[4,64,128]{2,1,0:T(8,128)S(1)}, s32[]{:T(128)}, f32[32,4]{1,0:T(8,128)S(1)}, f32[32,4,64,128]{3,2,1,0:T(8,128)}, ...), condition=%wide.region_3.4_spmd.clone, body=%wide.region_2.3_spmd.clone.sunk | while | flops 131076 | bytes 393369 | solution.py:32
  166.8 1.0 fusion.51
  167.9 1.0 fusion.51
  168.9 1.0 fusion.51
  172.0 1.0 fusion.51
  199.9 26.8 %psum.7 = f32[4,256]{1,0:T(4,128)S(1)} all-reduce(f32[4,256]{1,0:T(4,128)S(1)} %broadcast_select_fusion), channel_id=1, replica_groups=mesh['ctx'=32,'tp'=16] {'tp'}, use_global_device_ids=true, to_apply=%region_5.6 | all-reduce | flops 1024 | bytes 8192 | tf_op jit(solution)/shard_map/psum | solution.py:167
  226.9 1.8 fusion.26
  228.7 61.1 %reduce-scatter.2.cloned.1.call-done = f32[16,2048]{1,0:T(8,128)} async-done(((f32[256,2048]{1,0:T(8,128)}), f32[16,2048]{1,0:T(8,128)}) %reduce-scatter.2.cloned.1.call-update) | async-done | bytes 131088 | tf_op jit(solution)/shard_map/reduce_scatter | solution.py:171
  289.9 1.5 convert_element_type.77
  (165 shorter events, 37.5 us)
Async XLA Ops:
  6.5 220.3 %copy-start = (bf16[256,2048]{1,0:T(8,128)(2,1)S(1)}, bf16[256,2048]{1,0:T(8,128)(2,1)}, u32[]{:S(2)}) copy-start(bf16[256,2048]{1,0:T(8,128)(2,1)} %param.27) | copy-start | bytes 3145732
  6.5 56.9 %all-gather.5.cloned.1.call-start = ((), (), s32[]{:S(2)}) async-start(), calls=%async_computation.1 | async-start | bytes 4456448 | tf_op jit(solution)/shard_map/all_gather | solution.py:68
  8.5 157.3 %all-gather.7.cloned.1.call-start = ((), (), s32[]{:S(2)}) async-start(), calls=%async_computation.3 | async-start | bytes 4325376 | tf_op jit(solution)/shard_map/all_gather | solution.py:22
  8.5 8.4 %collective-permute-start = (bf16[16,2048]{1,0:T(8,128)(2,1)}, bf16[16,2048]{1,0:T(8,128)(2,1)S(1)}, u32[]{:S(2)}, u32[]{:S(2)}) collective-permute-start(bf16[16,2048]{1,0:T(8,128)(2,1)} %param.15), channel_id=1, source_target_pairs={{0,1},{1,2},{2,3},{3,4},{4,5},{5,6},{6,7},{7,8},{8,9},{9,10},{10,1... | collective-permute-start | bytes 196616 | tf_op jit(solution)/shard_map/ppermute | solution.py:83
  11.6 8.3 %collective-permute-start.1 = (bf16[16,2048]{1,0:T(8,128)(2,1)}, bf16[16,2048]{1,0:T(8,128)(2,1)S(1)}, u32[]{:S(2)}, u32[]{:S(2)}) collective-permute-start(bf16[16,2048]{1,0:T(8,128)(2,1)} %param.15), channel_id=1, source_target_pairs={{0,15},{1,0},{2,1},{3,2},{4,3},{5,4},{6,5},{7,6},{8,7},{9,8},{10,9... | collective-permute-start | bytes 196616 | tf_op jit(solution)/shard_map/ppermute | solution.py:88
  11.6 4.2 %copy-start.6 = (f32[4]{0:T(128)S(1)}, f32[4]{0:T(128)}, u32[]{:S(2)}) copy-start(f32[4]{0:T(128)} %param.24) | copy-start | bytes 52
  11.6 4.2 %copy-start.2 = (f32[4,256]{1,0:T(4,128)S(1)}, f32[4,256]{1,0:T(4,128)}, u32[]{:S(2)}) copy-start(f32[4,256]{1,0:T(4,128)} %param.19) | copy-start | bytes 12292
  11.6 4.4 %copy-start.1 = (bf16[16,2048]{1,0:T(8,128)(2,1)S(1)}, bf16[16,2048]{1,0:T(8,128)(2,1)}, u32[]{:S(2)}) copy-start(bf16[16,2048]{1,0:T(8,128)(2,1)} %param.15) | copy-start | bytes 196612
  15.0 39.7 %copy-start.5 = (bf16[2048,4]{0,1:T(4,128)(2,1)S(1)}, bf16[2048,4]{0,1:T(4,128)(2,1)}, u32[]{:S(2)}) copy-start(bf16[2048,4]{0,1:T(4,128)(2,1)} %param.17) | copy-start | bytes 49156
  15.0 39.7 %copy-start.7 = (f32[4]{0:T(128)S(1)}, f32[4]{0:T(128)}, u32[]{:S(2)}) copy-start(f32[4]{0:T(128)} %param.23) | copy-start | bytes 52
  16.9 4.3 %collective-permute-start.2 = (bf16[16,2048]{1,0:T(8,128)(2,1)S(1)}, bf16[16,2048]{1,0:T(8,128)(2,1)S(1)}, u32[]{:S(2)}, u32[]{:S(2)}) collective-permute-start(bf16[16,2048]{1,0:T(8,128)(2,1)S(1)} %collective-permute-done), channel_id=1, source_target_pairs={{0,1},{1,2},{2,3},{3,4},{4,5},{5,6},{6,7},{7,8},{8,9},{9,10},{10,1... | collective-permute-start | bytes 196616 | tf_op jit(solution)/shard_map/ppermute | solution.py:83
  19.9 4.9 %collective-permute-start.3 = (bf16[16,2048]{1,0:T(8,128)(2,1)S(1)}, bf16[16,2048]{1,0:T(8,128)(2,1)S(1)}, u32[]{:S(2)}, u32[]{:S(2)}) collective-permute-start(bf16[16,2048]{1,0:T(8,128)(2,1)S(1)} %collective-permute-done.1), channel_id=1, source_target_pairs={{0,15},{1,0},{2,1},{3,2},{4,3},{5,4},{6,5},{7,6},{8,7},{9,8},{10,9... | collective-permute-start | bytes 196616 | tf_op jit(solution)/shard_map/ppermute | solution.py:88
  21.2 4.9 %collective-permute-start.4 = (bf16[16,2048]{1,0:T(8,128)(2,1)S(1)}, bf16[16,2048]{1,0:T(8,128)(2,1)S(1)}, u32[]{:S(2)}, u32[]{:S(2)}) collective-permute-start(bf16[16,2048]{1,0:T(8,128)(2,1)S(1)} %collective-permute-done.2), channel_id=1, source_target_pairs={{0,1},{1,2},{2,3},{3,4},{4,5},{5,6},{6,7},{7,8},{8,9},{9,10},{10,1... | collective-permute-start | bytes 196616 | tf_op jit(solution)/shard_map/ppermute | solution.py:83
  24.8 4.9 %collective-permute-start.5 = (bf16[16,2048]{1,0:T(8,128)(2,1)S(1)}, bf16[16,2048]{1,0:T(8,128)(2,1)S(1)}, u32[]{:S(2)}, u32[]{:S(2)}) collective-permute-start(bf16[16,2048]{1,0:T(8,128)(2,1)S(1)} %collective-permute-done.3), channel_id=1, source_target_pairs={{0,15},{1,0},{2,1},{3,2},{4,3},{5,4},{6,5},{7,6},{8,7},{9,8},{10,9... | collective-permute-start | bytes 196616 | tf_op jit(solution)/shard_map/ppermute | solution.py:88
  26.1 6.0 %collective-permute-start.6 = (bf16[16,2048]{1,0:T(8,128)(2,1)S(1)}, bf16[16,2048]{1,0:T(8,128)(2,1)S(1)}, u32[]{:S(2)}, u32[]{:S(2)}) collective-permute-start(bf16[16,2048]{1,0:T(8,128)(2,1)S(1)} %collective-permute-done.4), channel_id=1, source_target_pairs={{0,1},{1,2},{2,3},{3,4},{4,5},{5,6},{6,7},{7,8},{8,9},{9,10},{10,1... | collective-permute-start | bytes 196616 | tf_op jit(solution)/shard_map/ppermute | solution.py:83
  29.7 6.7 %collective-permute-start.7 = (bf16[16,2048]{1,0:T(8,128)(2,1)S(1)}, bf16[16,2048]{1,0:T(8,128)(2,1)S(1)}, u32[]{:S(2)}, u32[]{:S(2)}) collective-permute-start(bf16[16,2048]{1,0:T(8,128)(2,1)S(1)} %collective-permute-done.5), channel_id=1, source_target_pairs={{0,15},{1,0},{2,1},{3,2},{4,3},{5,4},{6,5},{7,6},{8,7},{9,8},{10,9... | collective-permute-start | bytes 196616 | tf_op jit(solution)/shard_map/ppermute | solution.py:88
  32.2 5.1 %collective-permute-start.8 = (bf16[16,2048]{1,0:T(8,128)(2,1)S(1)}, bf16[16,2048]{1,0:T(8,128)(2,1)S(1)}, u32[]{:S(2)}, u32[]{:S(2)}) collective-permute-start(bf16[16,2048]{1,0:T(8,128)(2,1)S(1)} %collective-permute-done.6), channel_id=1, source_target_pairs={{0,1},{1,2},{2,3},{3,4},{4,5},{5,6},{6,7},{7,8},{8,9},{9,10},{10,1... | collective-permute-start | bytes 196616 | tf_op jit(solution)/shard_map/ppermute | solution.py:83
  36.4 6.6 %collective-permute-start.9 = (bf16[16,2048]{1,0:T(8,128)(2,1)S(1)}, bf16[16,2048]{1,0:T(8,128)(2,1)S(1)}, u32[]{:S(2)}, u32[]{:S(2)}) collective-permute-start(bf16[16,2048]{1,0:T(8,128)(2,1)S(1)} %collective-permute-done.7), channel_id=1, source_target_pairs={{0,15},{1,0},{2,1},{3,2},{4,3},{5,4},{6,5},{7,6},{8,7},{9,8},{10,9... | collective-permute-start | bytes 196616 | tf_op jit(solution)/shard_map/ppermute | solution.py:88
  37.2 5.9 %collective-permute-start.10 = (bf16[16,2048]{1,0:T(8,128)(2,1)S(1)}, bf16[16,2048]{1,0:T(8,128)(2,1)S(1)}, u32[]{:S(2)}, u32[]{:S(2)}) collective-permute-start(bf16[16,2048]{1,0:T(8,128)(2,1)S(1)} %collective-permute-done.8), channel_id=1, source_target_pairs={{0,1},{1,2},{2,3},{3,4},{4,5},{5,6},{6,7},{7,8},{8,9},{9,10},{10,1... | collective-permute-start | bytes 196616 | tf_op jit(solution)/shard_map/ppermute | solution.py:83
  42.9 6.2 %collective-permute-start.11 = (bf16[16,2048]{1,0:T(8,128)(2,1)S(1)}, bf16[16,2048]{1,0:T(8,128)(2,1)S(1)}, u32[]{:S(2)}, u32[]{:S(2)}) collective-permute-start(bf16[16,2048]{1,0:T(8,128)(2,1)S(1)} %collective-permute-done.9), channel_id=1, source_target_pairs={{0,15},{1,0},{2,1},{3,2},{4,3},{5,4},{6,5},{7,6},{8,7},{9,8},{10,9... | collective-permute-start | bytes 196616 | tf_op jit(solution)/shard_map/ppermute | solution.py:88
  43.1 6.0 %collective-permute-start.12 = (bf16[16,2048]{1,0:T(8,128)(2,1)S(1)}, bf16[16,2048]{1,0:T(8,128)(2,1)S(1)}, u32[]{:S(2)}, u32[]{:S(2)}) collective-permute-start(bf16[16,2048]{1,0:T(8,128)(2,1)S(1)} %collective-permute-done.10), channel_id=1, source_target_pairs={{0,1},{1,2},{2,3},{3,4},{4,5},{5,6},{6,7},{7,8},{8,9},{9,10},{10,1... | collective-permute-start | bytes 196616 | tf_op jit(solution)/shard_map/ppermute | solution.py:83
  49.1 5.6 %collective-permute-start.13 = (bf16[16,2048]{1,0:T(8,128)(2,1)S(1)}, bf16[16,2048]{1,0:T(8,128)(2,1)S(1)}, u32[]{:S(2)}, u32[]{:S(2)}) collective-permute-start(bf16[16,2048]{1,0:T(8,128)(2,1)S(1)} %collective-permute-done.11), channel_id=1, source_target_pairs={{0,15},{1,0},{2,1},{3,2},{4,3},{5,4},{6,5},{7,6},{8,7},{9,8},{10,9... | collective-permute-start | bytes 196616 | tf_op jit(solution)/shard_map/ppermute | solution.py:88
  49.2 5.5 %collective-permute-start.14 = (bf16[16,2048]{1,0:T(8,128)(2,1)S(1)}, bf16[16,2048]{1,0:T(8,128)(2,1)S(1)}, u32[]{:S(2)}, u32[]{:S(2)}) collective-permute-start(bf16[16,2048]{1,0:T(8,128)(2,1)S(1)} %collective-permute-done.12), channel_id=1, source_target_pairs={{0,1},{1,2},{2,3},{3,4},{4,5},{5,6},{6,7},{7,8},{8,9},{9,10},{10,1... | collective-permute-start | bytes 196616 | tf_op jit(solution)/shard_map/ppermute | solution.py:83
  59.0 9.3 %copy-start.4 = (f32[256]{0:T(256)S(1)}, f32[256]{0:T(256)}, u32[]{:S(2)}) copy-start(f32[256]{0:T(256)} %param.20) | copy-start | bytes 3076
  59.1 4.3 %collective-permute-start.15 = (bf16[3,256]{1,0:T(4,128)(2,1)S(1)}, bf16[3,256]{1,0:T(4,128)(2,1)S(1)}, u32[]{:S(2)}, u32[]{:S(2)}) collective-permute-start(bf16[3,256]{1,0:T(4,128)(2,1)S(1)} %slice.115), channel_id=1, source_target_pairs={{0,16},{16,32},{32,48},{48,64},{64,80},{80,96},{96,112},{112,128},... | collective-permute-start | bytes 4616 | tf_op jit(solution)/shard_map/ppermute | solution.py:17
  65.2 4.3 %collective-permute-start.16 = (bf16[3,256]{1,0:T(4,128)(2,1)S(1)}, bf16[3,256]{1,0:T(4,128)(2,1)S(1)}, u32[]{:S(2)}, u32[]{:S(2)}) collective-permute-start(bf16[3,256]{1,0:T(4,128)(2,1)S(1)} %slice.121), channel_id=1, source_target_pairs={{0,16},{16,32},{32,48},{48,64},{64,80},{80,96},{96,112},{112,128},... | collective-permute-start | bytes 4616 | tf_op jit(solution)/shard_map/ppermute | solution.py:17
  69.7 129.3 %copy-start.8 = (f32[4]{0:T(128)S(1)}, f32[4]{0:T(128)}, u32[]{:S(2)}) copy-start(f32[4]{0:T(128)} %param.25) | copy-start | bytes 52
  70.6 219.3 %reduce-scatter.2.cloned.1.call-start = ((), (), s32[]{:S(2)}) async-start(), calls=%async_computation.2 | async-start | bytes 2228224 | tf_op jit(solution)/shard_map/reduce_scatter | solution.py:171
  198.9 28.0 %copy-start.3 = (f32[256]{0:T(256)S(1)}, f32[256]{0:T(256)}, u32[]{:S(2)}) copy-start(f32[256]{0:T(256)} %param.26) | copy-start | bytes 3076
Sparse Core Ops, SparseCore 0:
  9.5 49.3 all-gather.4
  70.7 95.0 all-gather.6
  228.8 60.9 reduce-scatter.1
